TPU v7x, 256 devices: a whole 4x4x8 slice. The times are simulated.
256 devices in a mesh: row: 8 (over x, core), col: 32 (over z, y).
Axes of the slice: x: 4, y: 4, z: 8, core: 2. Of those that a mesh axis runs over, the one named last changes fastest.
Arguments:
- leaf_rhs: bfloat16 [6144, 128, 512], P(('row', 'col')), may hold values from -6 to 6
- leaf_inverse: bfloat16 [6144, 128, 128], P(('row', 'col')), as said below
- leaf_link: bfloat16 [6144, 128, 128], P(('row', 'col')), may hold values from -0.109375 to 0.109375
- leaf_parent: int32 [6144], P(('row', 'col')), may hold values from 0 to 255, as said below
- node_rhs: bfloat16 [256, 128, 512], P(('row', 'col')), may hold values from -6 to 6
- node_inverse: bfloat16 [256, 128, 128], P(('row', 'col')), as said below
- node_link: bfloat16 [256, 128, 128], P(('row', 'col')), may hold values from -0.25 to 0.25
- node_parent: int32 [256], P('row'), may hold values from 0 to 63, as said below
- middle_rhs: bfloat16 [64, 128, 512], P('row'), may hold values from -6 to 6
- middle_inverse: bfloat16 [64, 128, 128], P('row'), as said below
- middle_link: bfloat16 [64, 128, 128], P('row'), may hold values from -0.125 to 0.125
- middle_parent: int32 [64], P('row'), may hold values from 0 to 3
- top_rhs: bfloat16 [4, 128, 512], replicated, may hold values from -6 to 6
- top_inverse: bfloat16 [4, 128, 128], replicated, as said below
Outputs:
- leaf_result: bfloat16 [6144, 128, 512], P(('row', 'col'))
- node_result: bfloat16 [256, 128, 512], P(('row', 'col'))
- middle_result: bfloat16 [64, 128, 512], P('row')
- top_result: bfloat16 [4, 128, 512], replicated
Inputs may be any that keep to these rules, and one draw needn't show every extreme that they name: `leaf_parent`: the parent of a leaf held by the device at grid row r lies in block row r: it is r * 32 + c for some c below 32. `node_parent`: the parent of second-level supernode r * 32 + c is r * 8 + j for some j below 8. `leaf_inverse`: each block is lower triangular. `node_inverse`: each block is lower triangular. `middle_inverse`: each block is lower triangular. `top_inverse`: each block is lower triangular.
All inputs are finite; a program needn't handle non-finite values.
Results may differ from a plain program's by a relative error of at most 0.017.
Values may be sent and summed in bfloat16 or wider, within the bound.
No kernel may reach another device: no remote copies, remote signals or barrier semaphores. Data moves between devices by JAX's collectives and lax.ppermute only.
A program may use at most 128 MiB of HBM per device.

v0:
```python
import jax
import jax.numpy as jnp
from jax import lax
from jax.sharding import PartitionSpec as P


def apply_block(matrix, vectors):
    return jnp.einsum("nij,njr->nir", matrix, vectors, preferred_element_type=jnp.float32)


def apply_transposed(matrix, vectors):
    return jnp.einsum("nij,nir->njr", matrix, vectors, preferred_element_type=jnp.float32)


def slot_sums(targets, count, values):
    slots = lax.iota(jnp.int32, count)
    select = (slots[:, None] == targets[None, :]).astype(jnp.float32)
    return jnp.einsum("sk,kwr->swr", select, values, precision=lax.Precision.HIGHEST)


def local(
    leaf_rhs,
    leaf_inverse,
    leaf_link,
    leaf_parent,
    node_rhs,
    node_inverse,
    node_link,
    node_parent,
    middle_rhs,
    middle_inverse,
    middle_link,
    middle_parent,
    top_rhs,
    top_inverse,
):
    peers = lax.axis_size("col")
    col_index = lax.axis_index("col")
    middle_count = middle_rhs.shape[0]
    top_count = top_rhs.shape[0]
    leaf_target = leaf_parent % peers
    middle_target = node_parent % middle_count
    leaf_solved = apply_block(leaf_inverse, leaf_rhs).astype(jnp.bfloat16)
    leaf_update = apply_block(leaf_link, leaf_solved)
    node_sum = lax.psum_scatter(
        slot_sums(leaf_target, lax.axis_size("col") * 1, leaf_update),
        "col",
        scatter_dimension=0,
        tiled=True,
    )
    node_y = (node_rhs.astype(jnp.float32) - node_sum).astype(jnp.bfloat16)
    node_solved = apply_block(node_inverse, node_y).astype(jnp.bfloat16)
    own_target = lax.dynamic_slice_in_dim(middle_target, col_index, 1)
    middle_term = slot_sums(own_target, middle_count, apply_block(node_link, node_solved))
    middle_sum = lax.psum(middle_term, "col")
    middle_y = (middle_rhs.astype(jnp.float32) - middle_sum).astype(jnp.bfloat16)
    middle_solved = apply_block(middle_inverse, middle_y).astype(jnp.bfloat16)
    top_term = slot_sums(middle_parent, top_count, apply_block(middle_link, middle_solved))
    top_sum = lax.psum(top_term, "row")
    top_y = (top_rhs.astype(jnp.float32) - top_sum).astype(jnp.bfloat16)
    top_solved = apply_block(top_inverse, top_y).astype(jnp.bfloat16)
    top_result = apply_transposed(top_inverse, top_solved).astype(jnp.bfloat16)
    middle_w = (
        middle_solved.astype(jnp.float32) - apply_transposed(middle_link, top_result[middle_parent])
    ).astype(jnp.bfloat16)
    middle_result = apply_transposed(middle_inverse, middle_w).astype(jnp.bfloat16)
    node_w = (
        node_solved.astype(jnp.float32) - apply_transposed(node_link, middle_result[own_target])
    ).astype(jnp.bfloat16)
    node_result = apply_transposed(node_inverse, node_w).astype(jnp.bfloat16)
    row_result = lax.all_gather(node_result, "col", axis=0, tiled=True)
    leaf_w = (
        leaf_solved.astype(jnp.float32) - apply_transposed(leaf_link, row_result[leaf_target])
    ).astype(jnp.bfloat16)
    leaf_result = apply_transposed(leaf_inverse, leaf_w).astype(jnp.bfloat16)
    return (leaf_result, node_result, middle_result, top_result)


def solution(mesh):
    placed = (
        P(("row", "col"), None, None),
        P(("row", "col"), None, None),
        P(("row", "col"), None, None),
        P(("row", "col")),
        P(("row", "col"), None, None),
        P(("row", "col"), None, None),
        P(("row", "col"), None, None),
        P("row"),
        P("row", None, None),
        P("row", None, None),
        P("row", None, None),
        P("row"),
        P(),
        P(),
    )
    return jax.shard_map(
        local,
        mesh=mesh,
        in_specs=placed,
        out_specs=(
            P(("row", "col"), None, None),
            P(("row", "col"), None, None),
            P("row", None, None),
            P(),
        ),
        check_vma=False,
    )
```

profile of v0, /device:TPU:16, one launch (start us, length us, event | category | flops | bytes accessed | tf_op | source)
XLA Modules:
  0.0 620.0 jit_solution(1758936488983695656)
XLA Ops:
  7.2 0.0 copy-start
  7.2 0.0 reduce-scatter.2.cloned.1.call-start
  7.2 1.8 copy-done
  9.1 2.2 convolution_convert_fusion
  11.2 0.0 copy-start.2
  11.3 1.7 copy-done.2
  12.9 0.0 copy-done.3
  12.9 3.7 convolution_bitcast_fusion
  16.6 6.7 %copy.50 = f32[24,128,512]{2,0,1:T(8,128)} copy(f32[24,128,512]{1,2,0:T(8,128)} %convolution_bitcast_fusion) | data formatting | bytes 12582912 | tf_op jit(solution)/shard_map/nij,njr->nir/dot_general | solution.py:8
  23.3 0.0 copy-done.16
  23.3 7.5 %fusion.22 = f32[32,128,512]{2,0,1:T(8,128)S(1)} fusion(f32[24,128,512]{2,0,1:T(8,128)} %copy.50, s32[24]{0:T(128)S(1)} %get-tuple-element.32), kind=kOutput, calls=%fused_computation.35 | convolution fusion | flops 603980544 | bytes 14680160 | tf_op jit(solution)/shard_map/sk,kwr->swr/dot_general | solution.py:18
  30.9 8.1 %copy.51 = f32[32,128,512]{2,1,0:T(8,128)} copy(f32[32,128,512]{2,0,1:T(8,128)S(1)} %fusion.22) | data formatting | bytes 16777216 | tf_op jit(solution)/shard_map/sk,kwr->swr/dot_general | solution.py:18
  39.0 0.0 reduce-scatter.2.cloned.1.call-update
  39.0 0.0 copy-start.4
  39.0 0.0 copy-start.5
  39.0 0.0 all-reduce.3.cloned.1.call-start
  39.1 0.5 copy-done.17
  39.6 0.6 dynamic_slice.3
  40.2 0.6 compare_convert_fusion
  40.9 229.2 %reduce-scatter.2.cloned.1.call-done = f32[1,128,512]{2,1,0:T(8,128)} async-done(((f32[32,128,512]{2,1,0:T(8,128)}), f32[1,128,512]{2,1,0:T(8,128)}) %reduce-scatter.2.cloned.1.call-update) | async-done | bytes 262160 | tf_op jit(solution)/shard_map/reduce_scatter | solution.py:45
  270.1 0.0 copy-done.10
  270.1 0.0 copy-done.11
  270.1 1.2 convolution_convert_fusion.6
  271.3 0.0 copy-done.13
  271.3 0.2 convolution_bitcast_fusion.2
  271.5 0.1 copy.52
  271.6 1.6 broadcast_multiply_fusion
  273.3 0.0 all-reduce.3.cloned.1.call-update
  273.3 0.2 all-reduce.5.cloned.1.call-start
  273.5 152.5 %all-reduce.3.cloned.1.call-done = f32[8,128,512]{2,1,0:T(8,128)} async-done(((f32[8,128,512]{2,1,0:T(8,128)}), f32[8,128,512]{2,1,0:T(8,128)}) %all-reduce.3.cloned.1.call-update) | async-done | bytes 2097168 | tf_op jit(solution)/shard_map/psum | solution.py:55
  426.0 0.0 copy-done.4
  426.0 0.0 copy-done.5
  426.0 2.1 convolution_convert_fusion.2
  428.1 0.0 copy-done.6
  428.1 0.0 copy-start.15
  428.1 1.8 convolution_bitcast_fusion.1
  429.9 2.2 copy.54
  432.2 0.0 copy-done.15
  432.2 1.1 fusion.26
  433.3 0.0 copy-start.8
  433.3 0.0 copy-start.9
  433.3 1.3 copy.55
  434.6 0.0 all-reduce.5.cloned.1.call-update
  434.6 0.0 all-gather.3.cloned.1.call-start
  436.6 64.0 %all-reduce.5.cloned.1.call-done = f32[4,128,512]{2,1,0:T(8,128)} async-done(((f32[4,128,512]{2,1,0:T(8,128)}), f32[4,128,512]{2,1,0:T(8,128)}) %all-reduce.5.cloned.1.call-update) | async-done | bytes 1048592 | tf_op jit(solution)/shard_map/psum | solution.py:59
  500.7 0.0 copy-done.8
  500.7 0.0 copy-done.9
  500.7 1.7 fusion.7
  502.4 0.0 copy-start.12
  502.4 0.0 copy-start.14
  502.4 1.7 gather_fusion
  504.1 0.0 copy-done.7
  504.1 1.9 convolution_convert_fusion.1
  506.0 0.0 copy-done.12
  506.0 1.0 convolution_convert_fusion.5
  507.0 0.0 all-gather.3.cloned.1.call-update
  507.1 1.0 copy.64
  508.1 1.7 copy.62
  509.7 1.3 copy.63
  511.0 79.7 %all-gather.3.cloned.1.call-done = bf16[4096,512]{0,1:T(8,128)(2,1)} async-done(((bf16[128,512]{0,1:T(8,128)(2,1)}), bf16[4096,512]{0,1:T(8,128)(2,1)}) %all-gather.3.cloned.1.call-update) | async-done | bytes 4194320 | tf_op jit(solution)/shard_map/all_gather | solution.py:71
  590.7 6.5 %copy.71 = bf16[4096,512]{1,0:T(8,128)(2,1)} copy(bf16[4096,512]{0,1:T(8,128)(2,1)} %all-gather.3.cloned.1.call-done) | data formatting | bytes 8388608 | tf_op jit(solution)/shard_map/all_gather | solution.py:71
  597.2 4.7 gather_fusion.1
  601.9 6.9 %convert_bitcast_fusion = bf16[24,128,512]{1,2,0:T(8,128)(2,1)} fusion(bf16[24,128,128]{2,1,0:T(8,128)(2,1)} %param.15, bf16[24,128,512]{2,1,0:T(8,128)(2,1)} %copy-done.2, bf16[24,128,512]{2,1,0:T(8,128)(2,1)} %gather_fusion.1, bf16[24,128,128]{2,1,0:T(8,128)(2,1)} %param.16), kind=kOutput, calls=%fused_computation.5 | convolution fusion | flops 811597824 | bytes 11010048 | tf_op jit(solution)/shard_map/nij,nir->njr/dot_general | solution.py:12
  608.8 4.6 copy.61
  (16 shorter events, 0.1 us)
Async XLA Ops:
  7.2 1.9 copy-start
  7.2 262.9 %reduce-scatter.2.cloned.1.call-start = ((), (), s32[]{:S(2)}) async-start(), calls=%async_computation.1 | async-start | bytes 8650752 | tf_op jit(solution)/shard_map/reduce_scatter | solution.py:45
  9.1 3.8 copy-start.3
  11.2 1.7 copy-start.2
  16.6 6.7 %copy-start.16 = (s32[24]{0:T(128)S(1)}, s32[24]{0:T(128)}, u32[]{:S(2)}) copy-start(s32[24]{0:T(128)} %param.17) | copy-start | bytes 292
  39.0 0.7 copy-start.17
  39.0 231.1 %copy-start.10 = (bf16[1,128,512]{2,1,0:T(8,128)(2,1)S(1)}, bf16[1,128,512]{2,1,0:T(8,128)(2,1)}, u32[]{:S(2)}) copy-start(bf16[1,128,512]{2,1,0:T(8,128)(2,1)} %param.18) | copy-start | bytes 393220
  39.0 231.1 %copy-start.11 = (bf16[1,128,128]{2,1,0:T(8,128)(2,1)S(1)}, bf16[1,128,128]{2,1,0:T(8,128)(2,1)}, u32[]{:S(2)}) copy-start(bf16[1,128,128]{2,1,0:T(8,128)(2,1)} %param.19) | copy-start | bytes 98308
  39.0 232.3 %copy-start.13 = (bf16[1,128,128]{2,1,0:T(8,128)(2,1)S(1)}, bf16[1,128,128]{2,1,0:T(8,128)(2,1)}, u32[]{:S(2)}) copy-start(bf16[1,128,128]{2,1,0:T(8,128)(2,1)} %param.20) | copy-start | bytes 98308
  39.0 387.0 %copy-start.4 = (bf16[8,128,128]{2,1,0:T(8,128)(2,1)S(1)}, bf16[8,128,128]{2,1,0:T(8,128)(2,1)}, u32[]{:S(2)}) copy-start(bf16[8,128,128]{2,1,0:T(8,128)(2,1)} %param.23) | copy-start | bytes 786436
  39.0 387.0 %copy-start.5 = (bf16[8,128,512]{2,1,0:T(8,128)(2,1)S(1)}, bf16[8,128,512]{2,1,0:T(8,128)(2,1)}, u32[]{:S(2)}) copy-start(bf16[8,128,512]{2,1,0:T(8,128)(2,1)} %param.22) | copy-start | bytes 3145732
  39.0 387.0 %all-reduce.3.cloned.1.call-start = ((), (), s32[]{:S(2)}) async-start(), calls=%async_computation.2 | async-start | bytes 4194304 | tf_op jit(solution)/shard_map/psum | solution.py:55
  273.3 154.9 %copy-start.6 = (bf16[8,128,128]{2,1,0:T(8,128)(2,1)S(1)}, bf16[8,128,128]{2,1,0:T(8,128)(2,1)}, u32[]{:S(2)}) copy-start(bf16[8,128,128]{2,1,0:T(8,128)(2,1)} %param.24) | copy-start | bytes 786436
  273.3 227.4 %all-reduce.5.cloned.1.call-start = ((), (), s32[]{:S(2)}) async-start(), calls=%async_computation.3 | async-start | bytes 2097152 | tf_op jit(solution)/shard_map/psum | solution.py:59
  428.1 4.0 copy-start.15
  433.3 67.4 %copy-start.8 = (bf16[4,128,128]{2,1,0:T(8,128)(2,1)S(1)}, bf16[4,128,128]{2,1,0:T(8,128)(2,1)}, u32[]{:S(2)}) copy-start(bf16[4,128,128]{2,1,0:T(8,128)(2,1)} %param.27) | copy-start | bytes 393220
  433.3 67.4 %copy-start.9 = (bf16[4,128,512]{2,1,0:T(8,128)(2,1)S(1)}, bf16[4,128,512]{2,1,0:T(8,128)(2,1)}, u32[]{:S(2)}) copy-start(bf16[4,128,512]{2,1,0:T(8,128)(2,1)} %param.26) | copy-start | bytes 1572868
  434.6 69.5 %copy-start.7 = (bf16[8,128,128]{2,1,0:T(8,128)(2,1)S(1)}, bf16[8,128,128]{2,1,0:T(8,128)(2,1)}, u32[]{:S(2)}) copy-start(bf16[8,128,128]{2,1,0:T(8,128)(2,1)} %param.24) | copy-start | bytes 786436
  434.6 156.1 %all-gather.3.cloned.1.call-start = ((), (), s32[]{:S(2)}) async-start(), calls=%async_computation.4 | async-start | bytes 4325376 | tf_op jit(solution)/shard_map/all_gather | solution.py:71
  502.4 3.6 copy-start.12
  502.4 3.6 copy-start.14
  601.9 11.5 %copy-start.1 = (bf16[24,128,512]{2,1,0:T(8,128)(2,1)S(1)}, bf16[24,128,512]{2,1,0:T(8,128)(2,1)}, u32[]{:S(2)}) copy-start(bf16[24,128,512]{2,1,0:T(8,128)(2,1)} %param.14) | copy-start | bytes 9437188
Sparse Core Ops, SparseCore 0:
  39.1 230.9 reduce-scatter.1
  274.0 151.9 all-reduce.2
  434.7 65.9 all-reduce.4
  507.2 83.5 all-gather.2
where the time goes:
time: 621 us; the launch traced here: 620 us
  waiting for transfers between devices  525 us (85%)
  local copies, waits for them, and re-layouts  44.6 us (7%)
  matrix products  31.2 us (5%)
  between operations  16 us (3%)
    reduce_scatter x1, waiting for transfers between devices, local(): lax.psum_scatter(slot_sums(leaf_target, lax.axis_size('col') * 1, leaf_up...  229 us
    psum x1, waiting for transfers between devices, local(): middle_sum = lax.psum(middle_term, 'col')  152 us
    all_gather x1, waiting for transfers between devices, local(): row_result = lax.all_gather(node_result, 'col', axis=0, tiled=True)  79.7 us
    psum x1, waiting for transfers between devices, local(): top_sum = lax.psum(top_term, 'row')  64 us
    unnamed x40, local copies, waits for them, and re-layouts  12.7 us
  transfers between devices with their start and end apart: 4, of which 4 were waited for; matrix products, arithmetic and copies ran while one was open for 1% of the time, Pallas kernels for 0%

commit v1 on v0

--- a/solution.py
+++ b/solution.py
@@ -68,7 +68,9 @@
         node_solved.astype(jnp.float32) - apply_transposed(node_link, middle_result[own_target])
     ).astype(jnp.bfloat16)
     node_result = apply_transposed(node_inverse, node_w).astype(jnp.bfloat16)
-    row_result = lax.all_gather(node_result, "col", axis=0, tiled=True)
+    row_result = jnp.concatenate(
+        lax.all_to_all(jnp.stack([node_result] * lax.axis_size("col")), "col", 0, 0), axis=0
+    )
     leaf_w = (
         leaf_solved.astype(jnp.float32) - apply_transposed(leaf_link, row_result[leaf_target])
     ).astype(jnp.bfloat16)

time: 621 us -> 641 us (1.032)
  starting transfers between devices: 0.34 us -> 10.5 us
  waiting for transfers between devices: 525 us -> 535 us
    all_to_all x0 -> x1, waiting for transfers between devices: none -> 89.4 us  [local(): lax.all_to_all(jnp.stack([node_result] * lax.axis_size('col')), 'col', 0, 0)]
    all_gather x1 -> x0, waiting for transfers between devices: 79.7 us -> none  [local(): row_result = lax.all_gather(node_result, 'col', axis=0, tiled=True)]
    all_to_all x0 -> x1, starting transfers between devices: none -> 10.2 us  [local(): lax.all_to_all(jnp.stack([node_result] * lax.axis_size('col')), 'col', 0, 0)]
    all_gather x1 -> x0, local copies, waits for them, and re-layouts: 6.5 us -> none  [local(): row_result = lax.all_gather(node_result, 'col', axis=0, tiled=True)]
where the time goes in v1:
time: 641 us; the launch traced here: 635 us
  waiting for transfers between devices  535 us (83%)
  local copies, waits for them, and re-layouts  39.8 us (6%)
  matrix products  30.6 us (5%)
  between operations  16 us (2%)
  starting transfers between devices  10.5 us (2%)
    reduce_scatter x1, waiting for transfers between devices, local(): lax.psum_scatter(slot_sums(leaf_target, lax.axis_size('col') * 1, leaf_up...  229 us
    psum x1, waiting for transfers between devices, local(): middle_sum = lax.psum(middle_term, 'col')  153 us
    all_to_all x1, waiting for transfers between devices, local(): lax.all_to_all(jnp.stack([node_result] * lax.axis_size('col')), 'col', 0, 0)  89.4 us
    psum x1, waiting for transfers between devices, local(): top_sum = lax.psum(top_term, 'row')  64.1 us
  transfers between devices with their start and end apart: 4, of which 4 were waited for; matrix products, arithmetic and copies ran while one was open for 1% of the time, Pallas kernels for 0%

profile of v1, /device:TPU:16, one launch (start us, length us, event | category | flops | bytes accessed | tf_op | source)
XLA Modules:
  0.0 634.6 jit_solution(12836518238427122908)
XLA Ops:
  7.2 0.0 copy-start
  7.2 0.0 reduce-scatter.2.cloned.1.call-start
  7.2 1.8 copy-done
  9.1 2.2 convolution_convert_fusion
  11.2 0.0 copy-start.2
  11.3 1.7 copy-done.2
  12.9 0.0 copy-done.3
  12.9 3.7 convolution_bitcast_fusion
  16.6 6.7 %copy.82 = f32[24,128,512]{2,0,1:T(8,128)} copy(f32[24,128,512]{1,2,0:T(8,128)} %convolution_bitcast_fusion) | data formatting | bytes 12582912 | tf_op jit(solution)/shard_map/nij,njr->nir/dot_general | solution.py:8
  23.3 0.0 copy-done.16
  23.3 7.5 %fusion.22 = f32[32,128,512]{2,0,1:T(8,128)S(1)} fusion(f32[24,128,512]{2,0,1:T(8,128)} %copy.82, s32[24]{0:T(128)S(1)} %get-tuple-element.40), kind=kOutput, calls=%fused_computation.35 | convolution fusion | flops 603980544 | bytes 14680160 | tf_op jit(solution)/shard_map/sk,kwr->swr/dot_general | solution.py:18
  30.9 8.1 %copy.83 = f32[32,128,512]{2,1,0:T(8,128)} copy(f32[32,128,512]{2,0,1:T(8,128)S(1)} %fusion.22) | data formatting | bytes 16777216 | tf_op jit(solution)/shard_map/sk,kwr->swr/dot_general | solution.py:18
  39.0 0.0 reduce-scatter.2.cloned.1.call-update
  39.0 0.0 copy-start.4
  39.0 0.0 copy-start.5
  39.0 0.0 all-reduce.3.cloned.1.call-start
  39.1 0.5 copy-done.17
  39.6 0.6 dynamic_slice.3
  40.2 0.6 compare_convert_fusion
  40.9 229.4 %reduce-scatter.2.cloned.1.call-done = f32[1,128,512]{2,1,0:T(8,128)} async-done(((f32[32,128,512]{2,1,0:T(8,128)}), f32[1,128,512]{2,1,0:T(8,128)}) %reduce-scatter.2.cloned.1.call-update) | async-done | bytes 262160 | tf_op jit(solution)/shard_map/reduce_scatter | solution.py:45
  270.3 0.0 copy-done.10
  270.3 0.0 copy-done.11
  270.3 1.2 convolution_convert_fusion.6
  271.5 0.0 copy-done.13
  271.5 0.2 convolution_bitcast_fusion.2
  271.7 0.1 copy.84
  271.8 1.6 broadcast_multiply_fusion
  273.4 0.0 all-reduce.3.cloned.1.call-update
  273.5 0.2 all-reduce.5.cloned.1.call-start
  273.7 152.5 %all-reduce.3.cloned.1.call-done = f32[8,128,512]{2,1,0:T(8,128)} async-done(((f32[8,128,512]{2,1,0:T(8,128)}), f32[8,128,512]{2,1,0:T(8,128)}) %all-reduce.3.cloned.1.call-update) | async-done | bytes 2097168 | tf_op jit(solution)/shard_map/psum | solution.py:55
  426.2 0.0 copy-done.4
  426.2 0.0 copy-done.5
  426.2 2.1 convolution_convert_fusion.2
  428.3 0.0 copy-done.6
  428.3 0.0 copy-start.15
  428.3 1.8 convolution_bitcast_fusion.1
  430.1 2.2 copy.86
  432.4 0.0 copy-done.15
  432.4 1.1 fusion.26
  433.5 0.0 copy-start.8
  433.5 0.0 copy-start.9
  433.5 1.3 copy.87
  434.8 0.0 all-reduce.5.cloned.1.call-update
  436.8 64.1 %all-reduce.5.cloned.1.call-done = f32[4,128,512]{2,1,0:T(8,128)} async-done(((f32[4,128,512]{2,1,0:T(8,128)}), f32[4,128,512]{2,1,0:T(8,128)}) %all-reduce.5.cloned.1.call-update) | async-done | bytes 1048592 | tf_op jit(solution)/shard_map/psum | solution.py:59
  500.9 0.0 copy-done.9
  500.9 1.7 fusion.7
  502.6 0.0 copy-start.12
  502.6 0.0 copy-start.14
  502.6 1.7 gather_fusion
  504.3 1.9 convolution_convert_fusion.1
  506.2 0.0 copy-done.12
  506.2 0.0 copy-done.14
  506.2 0.3 convolution_convert_fusion.5
  506.5 0.1 copy.89
  506.7 2.5 stack.2
  509.1 10.2 %all-to-all-start = ((bf16[32,1,128,512]{3,2,1,0:T(8,128)(2,1)}), bf16[32,1,128,512]{3,2,1,0:T(8,128)(2,1)}, u32[]{:S(2)}, u32[]{:S(2)}) async-start(bf16[32,1,128,512]{3,2,1,0:T(8,128)(2,1)} %stack.2), calls=%async_computation.1 | async-start | bytes 8388608 | tf_op jit(solution)/shard_map/all_to_all | solution.py:72
  519.3 1.0 copy.96
  520.4 0.8 copy.94
  521.1 1.3 copy.95
  522.4 89.4 %all-to-all-done = bf16[32,1,128,512]{3,2,1,0:T(8,128)(2,1)} async-done(((bf16[32,1,128,512]{3,2,1,0:T(8,128)(2,1)}), bf16[32,1,128,512]{3,2,1,0:T(8,128)(2,1)}, u32[]{:S(2)}, u32[]{:S(2)}) %all-to-all-start) | async-done | bytes 4194336 | tf_op jit(solution)/shard_map/all_to_all | solution.py:72
  611.8 4.7 gather_fusion.1
  616.6 6.9 %convert_bitcast_fusion = bf16[24,128,512]{1,2,0:T(8,128)(2,1)} fusion(bf16[24,128,128]{2,1,0:T(8,128)(2,1)} %param.15, bf16[24,128,512]{2,1,0:T(8,128)(2,1)} %copy-done.2, bf16[24,128,512]{2,1,0:T(8,128)(2,1)} %gather_fusion.1, bf16[24,128,128]{2,1,0:T(8,128)(2,1)} %param.16), kind=kOutput, calls=%fused_computation.5 | convolution fusion | flops 811597824 | bytes 11010048 | tf_op jit(solution)/shard_map/nij,nir->njr/dot_general | solution.py:12
  623.5 4.6 copy.93
  628.1 0.0 copy-done.1
  (16 shorter events, 0.1 us)
Async XLA Ops:
  7.2 1.9 copy-start
  7.2 263.1 %reduce-scatter.2.cloned.1.call-start = ((), (), s32[]{:S(2)}) async-start(), calls=%async_computation.2 | async-start | bytes 8650752 | tf_op jit(solution)/shard_map/reduce_scatter | solution.py:45
  9.1 3.8 copy-start.3
  11.2 1.7 copy-start.2
  16.6 6.7 %copy-start.16 = (s32[24]{0:T(128)S(1)}, s32[24]{0:T(128)}, u32[]{:S(2)}) copy-start(s32[24]{0:T(128)} %param.17) | copy-start | bytes 292
  39.0 0.7 copy-start.17
  39.0 231.3 %copy-start.10 = (bf16[1,128,512]{2,1,0:T(8,128)(2,1)S(1)}, bf16[1,128,512]{2,1,0:T(8,128)(2,1)}, u32[]{:S(2)}) copy-start(bf16[1,128,512]{2,1,0:T(8,128)(2,1)} %param.18) | copy-start | bytes 393220
  39.0 231.3 %copy-start.11 = (bf16[1,128,128]{2,1,0:T(8,128)(2,1)S(1)}, bf16[1,128,128]{2,1,0:T(8,128)(2,1)}, u32[]{:S(2)}) copy-start(bf16[1,128,128]{2,1,0:T(8,128)(2,1)} %param.19) | copy-start | bytes 98308
  39.0 232.5 %copy-start.13 = (bf16[1,128,128]{2,1,0:T(8,128)(2,1)S(1)}, bf16[1,128,128]{2,1,0:T(8,128)(2,1)}, u32[]{:S(2)}) copy-start(bf16[1,128,128]{2,1,0:T(8,128)(2,1)} %param.20) | copy-start | bytes 98308
  39.0 387.2 %copy-start.4 = (bf16[8,128,128]{2,1,0:T(8,128)(2,1)S(1)}, bf16[8,128,128]{2,1,0:T(8,128)(2,1)}, u32[]{:S(2)}) copy-start(bf16[8,128,128]{2,1,0:T(8,128)(2,1)} %param.23) | copy-start | bytes 786436
  39.0 387.2 %copy-start.5 = (bf16[8,128,512]{2,1,0:T(8,128)(2,1)S(1)}, bf16[8,128,512]{2,1,0:T(8,128)(2,1)}, u32[]{:S(2)}) copy-start(bf16[8,128,512]{2,1,0:T(8,128)(2,1)} %param.22) | copy-start | bytes 3145732
  39.0 387.2 %all-reduce.3.cloned.1.call-start = ((), (), s32[]{:S(2)}) async-start(), calls=%async_computation.3 | async-start | bytes 4194304 | tf_op jit(solution)/shard_map/psum | solution.py:55
  273.4 154.9 %copy-start.6 = (bf16[8,128,128]{2,1,0:T(8,128)(2,1)S(1)}, bf16[8,128,128]{2,1,0:T(8,128)(2,1)}, u32[]{:S(2)}) copy-start(bf16[8,128,128]{2,1,0:T(8,128)(2,1)} %param.24) | copy-start | bytes 786436
  273.5 227.4 %all-reduce.5.cloned.1.call-start = ((), (), s32[]{:S(2)}) async-start(), calls=%async_computation.4 | async-start | bytes 2097152 | tf_op jit(solution)/shard_map/psum | solution.py:59
  428.3 4.0 copy-start.15
  433.5 67.4 %copy-start.8 = (bf16[4,128,128]{2,1,0:T(8,128)(2,1)S(1)}, bf16[4,128,128]{2,1,0:T(8,128)(2,1)}, u32[]{:S(2)}) copy-start(bf16[4,128,128]{2,1,0:T(8,128)(2,1)} %param.27) | copy-start | bytes 393220
  433.5 67.4 %copy-start.9 = (bf16[4,128,512]{2,1,0:T(8,128)(2,1)S(1)}, bf16[4,128,512]{2,1,0:T(8,128)(2,1)}, u32[]{:S(2)}) copy-start(bf16[4,128,512]{2,1,0:T(8,128)(2,1)} %param.26) | copy-start | bytes 1572868
  434.8 69.5 %copy-start.7 = (bf16[8,128,128]{2,1,0:T(8,128)(2,1)S(1)}, bf16[8,128,128]{2,1,0:T(8,128)(2,1)}, u32[]{:S(2)}) copy-start(bf16[8,128,128]{2,1,0:T(8,128)(2,1)} %param.24) | copy-start | bytes 786436
  502.6 3.6 copy-start.12
  502.6 3.6 copy-start.14
  509.1 102.7 %all-to-all-start = ((bf16[32,1,128,512]{3,2,1,0:T(8,128)(2,1)}), bf16[32,1,128,512]{3,2,1,0:T(8,128)(2,1)}, u32[]{:S(2)}, u32[]{:S(2)}) async-start(bf16[32,1,128,512]{3,2,1,0:T(8,128)(2,1)} %stack.2), calls=%async_computation.1 | async-start | bytes 8388608 | tf_op jit(solution)/shard_map/all_to_all | solution.py:72
  616.6 11.5 %copy-start.1 = (bf16[24,128,512]{2,1,0:T(8,128)(2,1)S(1)}, bf16[24,128,512]{2,1,0:T(8,128)(2,1)}, u32[]{:S(2)}) copy-start(bf16[24,128,512]{2,1,0:T(8,128)(2,1)} %param.14) | copy-start | bytes 9437188
Sparse Core Ops, SparseCore 0:
  39.1 231.0 reduce-scatter.1
  274.2 151.9 all-reduce.2
  434.9 65.9 all-reduce.4
